TPU v7x, 512 devices: a whole 4x8x8 slice. The times are simulated.
512 devices in a mesh: dp: 16 (over x, y_hi, core), tensor: 32 (over y_lo, z).
Axes of the slice: x: 4, y: 8 (y_hi: 2, y_lo: 4; y = y_hi * 4 + y_lo), z: 8, core: 2. Of those that a mesh axis runs over, the one named last changes fastest.
Arguments:
- tokens: bfloat16 [8192, 8192], P('dp', 'tensor'), may hold values from -6 to 6
- first_right: bfloat16 [32, 256, 1024], P('tensor'), may hold values from -0.375 to 0.375
- first_left: bfloat16 [128, 256, 256], P('tensor'), may hold values from -0.375 to 0.375
- second_right: bfloat16 [128, 256, 256], P('tensor'), may hold values from -0.375 to 0.375
- second_left: bfloat16 [32, 1024, 256], P('tensor'), may hold values from -0.1875 to 0.1875
- cotangent: bfloat16 [8192, 8192], P('dp', 'tensor'), may hold values from -6 to 6
Outputs:
- layer_out: bfloat16 [8192, 8192], P('dp', 'tensor')
- grad_tokens: bfloat16 [8192, 8192], P('dp', 'tensor')
- grad_first_right: float32 [32, 256, 1024], P('tensor', 'dp')
- grad_first_left: float32 [128, 256, 256], P('tensor', 'dp')
- grad_second_right: float32 [128, 256, 256], P('tensor', 'dp')
- grad_second_left: float32 [32, 1024, 256], P('tensor', 'dp')
All inputs are finite; a program needn't handle non-finite values.
Results may differ from a plain program's by a relative error of at most 0.018.
Values may be sent and summed in bfloat16 or wider, within the bound.
No kernel may reach another device: no remote copies, remote signals or barrier semaphores. Data moves between devices by JAX's collectives and lax.ppermute only.
A program may use at most 64 MiB of HBM per device.

v0:
```python
import jax
import jax.numpy as jnp
from jax import lax
from jax.sharding import PartitionSpec as P

half_root = 0.7071067811865476
inv_root_two_pi = 0.3989422804014327


def gelu_value(value):
    return 0.5 * value * (1.0 + jax.scipy.special.erf(value * half_root))


def gelu_slope(value):
    return (
        0.5 * (1.0 + jax.scipy.special.erf(value * half_root))
        + value * jnp.exp(-0.5 * value * value) * inv_root_two_pi
    )


def shards(tokens, first_right, first_left, second_right, second_left, cotangent):
    fp = jnp.float32
    bf = jnp.bfloat16
    tok_rows = tokens.shape[0]
    in_blocks = first_right.shape[0]
    block_width = first_right.shape[1]
    wide_width = first_right.shape[2]
    hid_blocks = first_left.shape[0]
    groups = lax.axis_size("tensor")
    replicas = lax.axis_size("dp")
    all_in = in_blocks * groups
    all_hid = hid_blocks * groups
    sub_width = wide_width // all_hid
    grad_scale = float(tok_rows * replicas) ** (-0.5)
    right_one = first_right.reshape(in_blocks, block_width, all_hid, sub_width)
    right_two = second_right.reshape(hid_blocks, block_width, all_in, sub_width)
    tok_parts = tokens.reshape(tok_rows, in_blocks, block_width)
    cot_parts = cotangent.reshape(tok_rows, in_blocks, block_width)
    up_inner = jnp.einsum("tkb,kbjg->jkgt", tok_parts, right_one, preferred_element_type=fp).astype(
        bf
    )
    arrived = lax.all_to_all(up_inner, "tensor", split_axis=0, concat_axis=1, tiled=True)
    mixed_piece = arrived.reshape(hid_blocks, block_width, arrived.shape[3])
    pre_piece = jnp.einsum("jbt,jbc->jct", mixed_piece, first_left, preferred_element_type=fp)
    hidden = gelu_value(pre_piece).astype(bf)
    down_inner = jnp.einsum("jbt,jbkg->kjgt", hidden, right_two, preferred_element_type=fp).astype(
        bf
    )
    mixed_down = lax.all_to_all(down_inner, "tensor", split_axis=0, concat_axis=1, tiled=True)
    mixed_down = mixed_down.reshape(in_blocks, wide_width, tok_rows)
    layer_out = jnp.einsum(
        "kwt,kwc->tkc", mixed_down, second_left, preferred_element_type=fp
    ).astype(bf)
    layer_out = layer_out.reshape(tok_rows, in_blocks * block_width)
    reduced = {}
    d_mixed_down = jnp.einsum(
        "tkc,kwc->kwt", cot_parts, second_left, preferred_element_type=fp
    ).astype(bf)
    d_mixed_down = d_mixed_down.reshape(in_blocks, all_hid, sub_width, tok_rows)
    d_down_inner = lax.all_to_all(d_mixed_down, "tensor", split_axis=1, concat_axis=0, tiled=True)
    d_hidden = jnp.einsum("kjgt,jbkg->jbt", d_down_inner, right_two, preferred_element_type=fp)
    d_pre = (d_hidden * gelu_slope(pre_piece)).astype(bf)
    d_mixed_up = jnp.einsum("jct,jbc->jbt", d_pre, first_left, preferred_element_type=fp).astype(bf)
    d_mixed_up = d_mixed_up.reshape(hid_blocks, all_in, sub_width, tok_rows)
    d_up_inner = lax.all_to_all(d_mixed_up, "tensor", split_axis=1, concat_axis=0, tiled=True)
    grad_tokens = jnp.einsum(
        "jkgt,kbjg->tkb", d_up_inner, right_one, preferred_element_type=fp
    ).astype(bf)
    grad_tokens = grad_tokens.reshape(tok_rows, in_blocks * block_width)
    result = jnp.einsum("jbt,kjgt->bjkg", hidden, d_down_inner, preferred_element_type=fp)
    term_result = jnp.einsum("tkb,jkgt->bkjg", tok_parts, d_up_inner, preferred_element_type=fp)
    summed = (
        lax.psum_scatter(
            (term_result.reshape(block_width, in_blocks, wide_width) * grad_scale).astype(
                jnp.bfloat16
            ),
            "dp",
            scatter_dimension=0,
            tiled=True,
        ).astype(jnp.float32),
        lax.psum_scatter(
            (
                jnp.einsum("jbt,jct->bjc", mixed_piece, d_pre, preferred_element_type=fp)
                * grad_scale
            ).astype(jnp.bfloat16),
            "dp",
            scatter_dimension=0,
            tiled=True,
        ).astype(jnp.float32),
        lax.psum_scatter(
            (result.reshape(block_width, hid_blocks, block_width) * grad_scale).astype(
                jnp.bfloat16
            ),
            "dp",
            scatter_dimension=0,
            tiled=True,
        ).astype(jnp.float32),
        lax.psum_scatter(
            (
                jnp.einsum("kwt,tkc->wkc", mixed_down, cot_parts, preferred_element_type=fp)
                * grad_scale
            ).astype(jnp.bfloat16),
            "dp",
            scatter_dimension=0,
            tiled=True,
        ).astype(jnp.float32),
    )
    reduced["right_one"] = summed[0]
    reduced["left_one"] = summed[1]
    reduced["right_two"] = summed[2]
    reduced["left_two"] = summed[3]
    grad_right_one = jnp.transpose(reduced["right_one"], (1, 0, 2))
    grad_left_one = jnp.transpose(reduced["left_one"], (1, 0, 2))
    grad_right_two = jnp.transpose(reduced["right_two"], (1, 0, 2))
    grad_left_two = jnp.transpose(reduced["left_two"], (1, 0, 2))
    return (layer_out, grad_tokens, grad_right_one, grad_left_one, grad_right_two, grad_left_two)


def solution(mesh):
    in_specs = (
        P("dp", "tensor"),
        P("tensor", None, None),
        P("tensor", None, None),
        P("tensor", None, None),
        P("tensor", None, None),
        P("dp", "tensor"),
    )
    out_specs = (
        P("dp", "tensor"),
        P("dp", "tensor"),
        P("tensor", "dp", None),
        P("tensor", "dp", None),
        P("tensor", "dp", None),
        P("tensor", "dp", None),
    )
    return jax.shard_map(shards, mesh=mesh, in_specs=in_specs, out_specs=out_specs, check_vma=False)
```

profile of v0, /device:TPU:1, one launch (start us, length us, event | category | flops | bytes accessed | tf_op | source)
XLA Modules:
  0.0 503.9 jit_solution(12077980124356621023)
XLA Ops:
  7.2 0.0 copy-start
  7.2 1.3 copy.71
  8.5 1.4 fusion.10
  9.9 1.6 copy.73
  11.5 14.3 %all-to-all-start = ((bf16[128,1,8,512]{3,2,1,0:T(8,128)(2,1)}), bf16[128,1,8,512]{3,2,1,0:T(8,128)(2,1)S(1)}, u32[]{:S(2)}, u32[]{:S(2)}) async-start(bf16[128,1,8,512]{3,2,1,0:T(8,128)(2,1)} %copy.73), calls=%async_computation | async-start | bytes 2097152 | tf_op jit(solution)/shard_map/all_to_all | solution.py:42
  25.8 1.5 fusion.11
  27.3 24.4 %all-to-all-done = bf16[128,1,8,512]{3,2,1,0:T(8,128)(2,1)S(1)} async-done(((bf16[128,1,8,512]{3,2,1,0:T(8,128)(2,1)}), bf16[128,1,8,512]{3,2,1,0:T(8,128)(2,1)S(1)}, u32[]{:S(2)}, u32[]{:S(2)}) %all-to-all-start) | async-done | bytes 1048608 | tf_op jit(solution)/shard_map/all_to_all | solution.py:42
  51.6 7.6 %all-to-all-start.2 = ((bf16[1,128,8,512]{3,2,0,1:T(8,128)(2,1)}), bf16[1,128,8,512]{3,2,0,1:T(8,128)(2,1)S(1)}, u32[]{:S(2)}, u32[]{:S(2)}) async-start(bf16[1,128,8,512]{3,2,0,1:T(8,128)(2,1)} %fusion.11), calls=%async_computation.2 | async-start | bytes 2097152 | tf_op jit(solution)/shard_map/all_to_all | solution.py:60
  59.2 2.0 copy.76
  61.3 0.5 fusion.25
  61.8 1.3 copy-done.1
  63.1 0.7 fusion.12
  63.9 1.5 copy.79
  65.4 19.5 %all-to-all-done.2 = bf16[1,128,8,512]{3,2,0,1:T(8,128)(2,1)S(1)} async-done(((bf16[1,128,8,512]{3,2,0,1:T(8,128)(2,1)}), bf16[1,128,8,512]{3,2,0,1:T(8,128)(2,1)S(1)}, u32[]{:S(2)}, u32[]{:S(2)}) %all-to-all-start.2) | async-done | bytes 1048608 | tf_op jit(solution)/shard_map/all_to_all | solution.py:60
  84.9 1.0 copy-done.3
  85.9 7.7 %all-to-all-start.1 = ((bf16[32,4,8,512]{3,2,1,0:T(8,128)(2,1)}), bf16[32,4,8,512]{3,2,1,0:T(8,128)(2,1)S(1)}, u32[]{:S(2)}, u32[]{:S(2)}) async-start(bf16[32,4,8,512]{3,2,1,0:T(8,128)(2,1)} %copy.79), calls=%async_computation.1 | async-start | bytes 2097152 | tf_op jit(solution)/shard_map/all_to_all | solution.py:49
  93.7 3.2 fusion.5
  96.9 0.5 fusion.13
  97.4 0.5 copy-done.2
  97.9 1.1 copy.83
  99.0 20.4 %all-to-all-done.1 = bf16[32,4,8,512]{3,2,1,0:T(8,128)(2,1)S(1)} async-done(((bf16[32,4,8,512]{3,2,1,0:T(8,128)(2,1)}), bf16[32,4,8,512]{3,2,1,0:T(8,128)(2,1)S(1)}, u32[]{:S(2)}, u32[]{:S(2)}) %all-to-all-start.1) | async-done | bytes 1048608 | tf_op jit(solution)/shard_map/all_to_all | solution.py:49
  119.4 7.9 %all-to-all-start.3 = ((bf16[4,32,8,512]{3,2,0,1:T(8,128)(2,1)}), bf16[4,32,8,512]{3,2,0,1:T(8,128)(2,1)}, u32[]{:S(2)}, u32[]{:S(2)}) async-start(bf16[4,32,8,512]{3,2,0,1:T(8,128)(2,1)} %copy.83), calls=%async_computation.3 | async-start | bytes 2097152 | tf_op jit(solution)/shard_map/all_to_all | solution.py:65
  127.2 0.0 reduce-scatter.3.cloned.1.call-start
  127.3 3.4 fusion.20
  130.7 2.0 copy.91
  132.7 0.0 reduce-scatter.3.cloned.1.call-update
  132.7 0.0 reduce-scatter.5.cloned.1.call-start
  132.8 1.3 dynamic-slice
  134.7 1.3 fusion.18
  136.0 0.0 reduce-scatter.5.cloned.1.call-update
  136.0 0.0 all-reduce.5.cloned.1.call-start
  136.1 2.6 fusion.21
  138.6 2.1 copy.88
  140.7 74.1 %reduce-scatter.3.cloned.1.call-done = bf16[16,4,256]{2,0,1:T(8,128)(2,1)} async-done(((bf16[256,4,256]{2,0,1:T(8,128)(2,1)}), bf16[16,4,256]{2,0,1:T(8,128)(2,1)}) %reduce-scatter.3.cloned.1.call-update) | async-done | bytes 32784 | tf_op jit(solution)/shard_map/reduce_scatter | solution.py:90
  214.8 1.4 convert_bitcast_fusion
  216.2 2.0 fusion.19
  218.3 0.3 copy.122
  218.6 2.1 copy.86
  220.7 1.2 convolution_convert_fusion.4
  221.9 0.0 all-reduce.5.cloned.1.call-update
  221.9 2.5 fusion.22
  224.3 76.8 %reduce-scatter.5.cloned.1.call-done = bf16[64,1,256]{2,0,1:T(8,128)(2,1)} async-done(((bf16[1024,1,256]{2,0,1:T(8,128)(2,1)}), bf16[64,1,256]{2,0,1:T(8,128)(2,1)}) %reduce-scatter.5.cloned.1.call-update) | async-done | bytes 32784 | tf_op jit(solution)/shard_map/reduce_scatter | solution.py:98
  301.1 1.4 bitcast_convert_fusion.1
  302.5 191.9 %all-reduce.5.cloned.1.call-done = (bf16[256,1,1024]{2,1,0:T(2,128)(2,1)}, bf16[256,4,256]{2,1,0:T(4,128)(2,1)}) async-done(((bf16[256,1,1024]{2,1,0:T(2,128)(2,1)}, bf16[256,4,256]{2,1,0:T(4,128)(2,1)}), (bf16[256,1,1024]{2,1,0:T(2,128)(2,1)}, bf16[256,4,256]{2,1,0:T(4,128)(2,1)})) %all-reduce.5.cloned.1.call-update) | async-done | bytes 1048592
  494.4 0.9 bitcast_convert_fusion
  495.3 0.8 convert_bitcast_fusion.1
  496.1 0.6 copy.93
  496.7 0.6 copy.92
  (15 shorter events, 0.0 us)
Async XLA Ops:
  7.2 54.1 %copy-start = (bf16[4,256,256]{2,1,0:T(8,128)(2,1)S(1)}, bf16[4,256,256]{2,1,0:T(8,128)(2,1)}, u32[]{:S(2)}) copy-start(bf16[4,256,256]{2,1,0:T(8,128)(2,1)} %param.8) | copy-start | bytes 1572868
  9.9 15.9 %copy-start.4 = (bf16[1,1024,256]{2,1,0:T(8,128)(2,1)S(1)}, bf16[1,1024,256]{2,1,0:T(8,128)(2,1)}, u32[]{:S(2)}) copy-start(bf16[1,1024,256]{2,1,0:T(8,128)(2,1)} %param.10) | copy-start | bytes 1572868
  9.9 15.9 %copy-start.7 = (bf16[512,256]{1,0:T(8,128)(2,1)S(1)}, bf16[512,256]{1,0:T(8,128)(2,1)}, u32[]{:S(2)}) copy-start(bf16[512,256]{1,0:T(8,128)(2,1)} %param.11) | copy-start | bytes 786436
  11.5 40.1 %all-to-all-start = ((bf16[128,1,8,512]{3,2,1,0:T(8,128)(2,1)}), bf16[128,1,8,512]{3,2,1,0:T(8,128)(2,1)S(1)}, u32[]{:S(2)}, u32[]{:S(2)}) async-start(bf16[128,1,8,512]{3,2,1,0:T(8,128)(2,1)} %copy.73), calls=%async_computation | async-start | bytes 2097152 | tf_op jit(solution)/shard_map/all_to_all | solution.py:42
  51.6 33.3 %all-to-all-start.2 = ((bf16[1,128,8,512]{3,2,0,1:T(8,128)(2,1)}), bf16[1,128,8,512]{3,2,0,1:T(8,128)(2,1)S(1)}, u32[]{:S(2)}, u32[]{:S(2)}) async-start(bf16[1,128,8,512]{3,2,0,1:T(8,128)(2,1)} %fusion.11), calls=%async_computation.2 | async-start | bytes 2097152 | tf_op jit(solution)/shard_map/all_to_all | solution.py:60
  61.3 1.9 copy-start.6
  61.8 1.3 copy-start.1
  84.9 1.0 copy-start.3
  85.9 33.4 %all-to-all-start.1 = ((bf16[32,4,8,512]{3,2,1,0:T(8,128)(2,1)}), bf16[32,4,8,512]{3,2,1,0:T(8,128)(2,1)S(1)}, u32[]{:S(2)}, u32[]{:S(2)}) async-start(bf16[32,4,8,512]{3,2,1,0:T(8,128)(2,1)} %copy.79), calls=%async_computation.1 | async-start | bytes 2097152 | tf_op jit(solution)/shard_map/all_to_all | solution.py:49
  96.9 1.0 copy-start.2
  119.4 96.8 %all-to-all-start.3 = ((bf16[4,32,8,512]{3,2,0,1:T(8,128)(2,1)}), bf16[4,32,8,512]{3,2,0,1:T(8,128)(2,1)}, u32[]{:S(2)}, u32[]{:S(2)}) async-start(bf16[4,32,8,512]{3,2,0,1:T(8,128)(2,1)} %copy.83), calls=%async_computation.3 | async-start | bytes 2097152 | tf_op jit(solution)/shard_map/all_to_all | solution.py:65
  127.2 87.6 %reduce-scatter.3.cloned.1.call-start = ((), (), s32[]{:S(2)}) async-start(), calls=%async_computation.6 | async-start | bytes 557056 | tf_op jit(solution)/shard_map/reduce_scatter | solution.py:90
  132.7 168.4 %reduce-scatter.5.cloned.1.call-start = ((), (), s32[]{:S(2)}) async-start(), calls=%async_computation.7 | async-start | bytes 557056 | tf_op jit(solution)/shard_map/reduce_scatter | solution.py:98
  136.0 80.2 %copy-start.8 = (bf16[512,256]{1,0:T(8,128)(2,1)S(1)}, bf16[512,256]{1,0:T(8,128)(2,1)}, u32[]{:S(2)}) copy-start(bf16[512,256]{1,0:T(8,128)(2,1)} %param.6) | copy-start | bytes 786436
  136.0 358.4 %all-reduce.5.cloned.1.call-start = ((), (), s32[]{:S(2)}) async-start(), calls=%async_computation.8 | async-start | bytes 3145728
  216.2 4.5 copy-start.5
Sparse Core Ops, SparseCore 0:
  132.9 81.9 reduce-scatter.2
  219.4 81.6 reduce-scatter.4
  304.1 190.2 all-reduce.4
where the time goes:
time: 505 us; the launch traced here: 504 us
  waiting for transfers between devices  407 us (81%)
  starting transfers between devices  37.6 us (7%)
  matrix products  20.7 us (4%)
  local copies, waits for them, and re-layouts  19.5 us (4%)
  between operations  14.6 us (3%)
    unnamed x4, waiting for transfers between devices  192 us
    reduce_scatter x1, waiting for transfers between devices, shards(): lax.psum_scatter((jnp.einsum('kwt,tkc->wkc', mixed_down, cot_parts, prefe...  76.8 us
    reduce_scatter x1, waiting for transfers between devices, shards(): lax.psum_scatter((result.reshape(block_width, hid_blocks, block_width) *...  74.1 us
    all_to_all x1, waiting for transfers between devices, shards(): lax.all_to_all(up_inner, 'tensor', split_axis=0, concat_axis=1, tiled=True)  24.4 us
    all_to_all x1, waiting for transfers between devices, shards(): lax.all_to_all(down_inner, 'tensor', split_axis=0, concat_axis=1, tiled=T...  20.4 us
    all_to_all x1, waiting for transfers between devices, shards(): lax.all_to_all(d_mixed_down, 'tensor', split_axis=1, concat_axis=0, tiled...  19.5 us
    all_to_all x1, starting transfers between devices, shards(): lax.all_to_all(up_inner, 'tensor', split_axis=0, concat_axis=1, tiled=True)  14.3 us
  transfers between devices with their start and end apart: 7, of which 6 were waited for; matrix products, arithmetic and copies ran while one was open for 7% of the time, Pallas kernels for 0%

commit v1 on v0

--- a/solution.py
+++ b/solution.py
@@ -1,3 +1,4 @@
+import functools
 import jax
 import jax.numpy as jnp
 from jax import lax
@@ -5,6 +6,22 @@
 
 half_root = 0.7071067811865476
 inv_root_two_pi = 0.3989422804014327
+
+
+def _load_shapes(point, axis_key):
+    u1 = jnp.concatenate(
+        jax.lax.all_to_all(
+            jnp.stack(jnp.split(point, jax.lax.psum(1, axis_name=axis_key), axis=0), axis=0),
+            axis_key,
+            0,
+            0,
+        ),
+        axis=1,
+    )
+    return u1
+
+
+lift_plane = functools.partial(_load_shapes, axis_key="tensor")
 
 
 def gelu_value(value):
@@ -39,7 +56,7 @@
     up_inner = jnp.einsum("tkb,kbjg->jkgt", tok_parts, right_one, preferred_element_type=fp).astype(
         bf
     )
-    arrived = lax.all_to_all(up_inner, "tensor", split_axis=0, concat_axis=1, tiled=True)
+    arrived = lift_plane(up_inner)
     mixed_piece = arrived.reshape(hid_blocks, block_width, arrived.shape[3])
     pre_piece = jnp.einsum("jbt,jbc->jct", mixed_piece, first_left, preferred_element_type=fp)
     hidden = gelu_value(pre_piece).astype(bf)

time: 505 us -> 523 us (1.036)
  local copies, waits for them, and re-layouts: 19.5 us -> 37.7 us
    unnamed x23 -> x54, local copies, waits for them, and re-layouts: 8.76 us -> 27.9 us
where the time goes in v1:
time: 523 us; the launch traced here: 522 us
  waiting for transfers between devices  407 us (78%)
  local copies, waits for them, and re-layouts  37.7 us (7%)
  starting transfers between devices  37.7 us (7%)
  matrix products  20.8 us (4%)
  between operations  14.6 us (3%)
    unnamed x4, waiting for transfers between devices  192 us
    reduce_scatter x1, waiting for transfers between devices, shards(): lax.psum_scatter((jnp.einsum('kwt,tkc->wkc', mixed_down, cot_parts, prefe...  76.8 us
    reduce_scatter x1, waiting for transfers between devices, shards(): lax.psum_scatter((result.reshape(block_width, hid_blocks, block_width) *...  73.9 us
    unnamed x54, local copies, waits for them, and re-layouts  27.9 us
    all_to_all x1, waiting for transfers between devices, _load_shapes(): jax.lax.all_to_all(jnp.stack(jnp.split(point, jax.lax.psum(1, axis_name=a...  24.4 us
    all_to_all x1, waiting for transfers between devices, shards(): lax.all_to_all(down_inner, 'tensor', split_axis=0, concat_axis=1, tiled=T...  20.4 us
    all_to_all x1, waiting for transfers between devices, shards(): lax.all_to_all(d_mixed_down, 'tensor', split_axis=1, concat_axis=0, tiled...  19.5 us
    all_to_all x1, starting transfers between devices, _load_shapes(): jax.lax.all_to_all(jnp.stack(jnp.split(point, jax.lax.psum(1, axis_name=a...  14.3 us
  transfers between devices with their start and end apart: 7, of which 6 were waited for; matrix products, arithmetic and copies ran while one was open for 7% of the time, Pallas kernels for 0%

profile of v1, /device:TPU:1, one launch (start us, length us, event | category | flops | bytes accessed | tf_op | source)
XLA Modules:
  0.0 521.9 jit_solution(12103484247657466501)
XLA Ops:
  7.2 1.3 copy.49
  8.5 1.4 convolution_convert_fusion.1
  9.9 0.6 constant_dynamic-update-slice_fusion.31
  10.6 0.6 constant_dynamic-update-slice_fusion.30
  14.3 0.6 constant_dynamic-update-slice_fusion.24
  15.5 0.6 constant_dynamic-update-slice_fusion.22
  16.8 0.6 constant_dynamic-update-slice_fusion.20
  20.4 0.6 constant_dynamic-update-slice_fusion.14
  22.3 0.6 constant_dynamic-update-slice_fusion.11
  22.9 0.6 constant_dynamic-update-slice_fusion.10
  24.2 0.6 constant_dynamic-update-slice_fusion.8
  25.4 0.6 constant_dynamic-update-slice_fusion.6
  26.7 0.6 constant_dynamic-update-slice_fusion.4
  27.9 0.6 constant_dynamic-update-slice_fusion.2
  29.8 14.3 %all-to-all-start = ((bf16[32,4,1,8,512]{4,1,3,2,0:T(4,128)(2,1)}), bf16[32,4,1,8,512]{4,1,3,2,0:T(4,128)(2,1)S(1)}, u32[]{:S(2)}, u32[]{:S(2)}) async-start(bf16[32,4,1,8,512]{4,1,3,2,0:T(4,128)(2,1)} %constant_dynamic-update-slice_fusion), calls=%async_computation | async-start | bytes 2097152 | tf_op jit(solution)/shard_map/all_to_all | solution.py:13
  44.1 1.5 fusion.10
  45.5 24.4 %all-to-all-done = bf16[32,4,1,8,512]{4,1,3,2,0:T(4,128)(2,1)S(1)} async-done(((bf16[32,4,1,8,512]{4,1,3,2,0:T(4,128)(2,1)}), bf16[32,4,1,8,512]{4,1,3,2,0:T(4,128)(2,1)S(1)}, u32[]{:S(2)}, u32[]{:S(2)}) %all-to-all-start) | async-done | bytes 1048608 | tf_op jit(solution)/shard_map/all_to_all | solution.py:13
  69.9 7.5 %all-to-all-start.2 = ((bf16[1,128,8,512]{3,2,0,1:T(8,128)(2,1)}), bf16[1,128,8,512]{3,2,0,1:T(8,128)(2,1)S(1)}, u32[]{:S(2)}, u32[]{:S(2)}) async-start(bf16[1,128,8,512]{3,2,0,1:T(8,128)(2,1)} %fusion.10), calls=%async_computation.2 | async-start | bytes 2097152 | tf_op jit(solution)/shard_map/all_to_all | solution.py:77
  77.5 2.0 copy.52
  80.1 1.3 copy-done.1
  81.4 0.7 fusion.11
  82.1 1.5 copy.55
  83.7 19.5 %all-to-all-done.2 = bf16[1,128,8,512]{3,2,0,1:T(8,128)(2,1)S(1)} async-done(((bf16[1,128,8,512]{3,2,0,1:T(8,128)(2,1)}), bf16[1,128,8,512]{3,2,0,1:T(8,128)(2,1)S(1)}, u32[]{:S(2)}, u32[]{:S(2)}) %all-to-all-start.2) | async-done | bytes 1048608 | tf_op jit(solution)/shard_map/all_to_all | solution.py:77
  103.2 1.0 copy-done.3
  104.2 7.7 %all-to-all-start.1 = ((bf16[32,4,8,512]{3,2,1,0:T(8,128)(2,1)}), bf16[32,4,8,512]{3,2,1,0:T(8,128)(2,1)S(1)}, u32[]{:S(2)}, u32[]{:S(2)}) async-start(bf16[32,4,8,512]{3,2,1,0:T(8,128)(2,1)} %copy.55), calls=%async_computation.1 | async-start | bytes 2097152 | tf_op jit(solution)/shard_map/all_to_all | solution.py:66
  111.9 3.2 fusion.5
  116.1 1.1 copy.59
  117.2 20.4 %all-to-all-done.1 = bf16[32,4,8,512]{3,2,1,0:T(8,128)(2,1)S(1)} async-done(((bf16[32,4,8,512]{3,2,1,0:T(8,128)(2,1)}), bf16[32,4,8,512]{3,2,1,0:T(8,128)(2,1)S(1)}, u32[]{:S(2)}, u32[]{:S(2)}) %all-to-all-start.1) | async-done | bytes 1048608 | tf_op jit(solution)/shard_map/all_to_all | solution.py:66
  137.6 7.9 %all-to-all-start.3 = ((bf16[4,32,8,512]{3,2,0,1:T(8,128)(2,1)}), bf16[4,32,8,512]{3,2,0,1:T(8,128)(2,1)}, u32[]{:S(2)}, u32[]{:S(2)}) async-start(bf16[4,32,8,512]{3,2,0,1:T(8,128)(2,1)} %copy.59), calls=%async_computation.3 | async-start | bytes 2097152 | tf_op jit(solution)/shard_map/all_to_all | solution.py:82
  145.5 3.4 fusion.19
  148.9 2.0 copy.68
  151.0 1.3 dynamic-slice
  153.0 1.3 fusion.17
  154.5 2.6 fusion.20
  157.1 2.1 copy.65
  159.2 73.9 %reduce-scatter.3.cloned.1.call-done = bf16[16,4,256]{2,0,1:T(8,128)(2,1)} async-done(((bf16[256,4,256]{2,0,1:T(8,128)(2,1)}), bf16[16,4,256]{2,0,1:T(8,128)(2,1)}) %reduce-scatter.3.cloned.1.call-update) | async-done | bytes 32784 | tf_op jit(solution)/shard_map/reduce_scatter | solution.py:107
  233.1 1.4 convert_bitcast_fusion
  234.5 2.0 fusion.18
  236.8 2.1 copy.62
  238.9 1.2 convolution_convert_fusion.4
  240.1 2.5 fusion.21
  242.6 76.8 %reduce-scatter.5.cloned.1.call-done = bf16[64,1,256]{2,0,1:T(8,128)(2,1)} async-done(((bf16[1024,1,256]{2,0,1:T(8,128)(2,1)}), bf16[64,1,256]{2,0,1:T(8,128)(2,1)}) %reduce-scatter.5.cloned.1.call-update) | async-done | bytes 32784 | tf_op jit(solution)/shard_map/reduce_scatter | solution.py:115
  319.4 1.4 bitcast_convert_fusion.1
  320.8 191.6 %all-reduce.5.cloned.1.call-done = (bf16[256,1,1024]{2,1,0:T(2,128)(2,1)}, bf16[256,4,256]{2,1,0:T(4,128)(2,1)}) async-done(((bf16[256,1,1024]{2,1,0:T(2,128)(2,1)}, bf16[256,4,256]{2,1,0:T(4,128)(2,1)}), (bf16[256,1,1024]{2,1,0:T(2,128)(2,1)}, bf16[256,4,256]{2,1,0:T(4,128)(2,1)})) %all-reduce.5.cloned.1.call-update) | async-done | bytes 1048592
  512.4 0.9 bitcast_convert_fusion
  513.3 0.8 convert_bitcast_fusion.1
  514.1 0.6 copy.70
  514.7 0.6 copy.69
  (46 shorter events, 14.5 us)
Async XLA Ops:
  7.2 72.4 %copy-start = (bf16[4,256,256]{2,1,0:T(8,128)(2,1)S(1)}, bf16[4,256,256]{2,1,0:T(8,128)(2,1)}, u32[]{:S(2)}) copy-start(bf16[4,256,256]{2,1,0:T(8,128)(2,1)} %param.8) | copy-start | bytes 1572868
  9.9 34.1 %copy-start.4 = (bf16[1,1024,256]{2,1,0:T(8,128)(2,1)S(1)}, bf16[1,1024,256]{2,1,0:T(8,128)(2,1)}, u32[]{:S(2)}) copy-start(bf16[1,1024,256]{2,1,0:T(8,128)(2,1)} %param.10) | copy-start | bytes 1572868
  9.9 34.1 %copy-start.7 = (bf16[512,256]{1,0:T(8,128)(2,1)S(1)}, bf16[512,256]{1,0:T(8,128)(2,1)}, u32[]{:S(2)}) copy-start(bf16[512,256]{1,0:T(8,128)(2,1)} %param.11) | copy-start | bytes 786436
  29.8 40.2 %all-to-all-start = ((bf16[32,4,1,8,512]{4,1,3,2,0:T(4,128)(2,1)}), bf16[32,4,1,8,512]{4,1,3,2,0:T(4,128)(2,1)S(1)}, u32[]{:S(2)}, u32[]{:S(2)}) async-start(bf16[32,4,1,8,512]{4,1,3,2,0:T(4,128)(2,1)} %constant_dynamic-update-slice_fusion), calls=%async_computation | async-start | bytes 2097152 | tf_op jit(solution)/shard_map/all_to_all | solution.py:13
  69.9 33.2 %all-to-all-start.2 = ((bf16[1,128,8,512]{3,2,0,1:T(8,128)(2,1)}), bf16[1,128,8,512]{3,2,0,1:T(8,128)(2,1)S(1)}, u32[]{:S(2)}, u32[]{:S(2)}) async-start(bf16[1,128,8,512]{3,2,0,1:T(8,128)(2,1)} %fusion.10), calls=%async_computation.2 | async-start | bytes 2097152 | tf_op jit(solution)/shard_map/all_to_all | solution.py:77
  79.5 1.9 copy-start.6
  80.1 1.3 copy-start.1
  103.2 1.0 copy-start.3
  104.2 33.4 %all-to-all-start.1 = ((bf16[32,4,8,512]{3,2,1,0:T(8,128)(2,1)}), bf16[32,4,8,512]{3,2,1,0:T(8,128)(2,1)S(1)}, u32[]{:S(2)}, u32[]{:S(2)}) async-start(bf16[32,4,8,512]{3,2,1,0:T(8,128)(2,1)} %copy.55), calls=%async_computation.1 | async-start | bytes 2097152 | tf_op jit(solution)/shard_map/all_to_all | solution.py:66
  115.1 1.0 copy-start.2
  137.6 96.8 %all-to-all-start.3 = ((bf16[4,32,8,512]{3,2,0,1:T(8,128)(2,1)}), bf16[4,32,8,512]{3,2,0,1:T(8,128)(2,1)}, u32[]{:S(2)}, u32[]{:S(2)}) async-start(bf16[4,32,8,512]{3,2,0,1:T(8,128)(2,1)} %copy.59), calls=%async_computation.3 | async-start | bytes 2097152 | tf_op jit(solution)/shard_map/all_to_all | solution.py:82
  145.5 87.6 %reduce-scatter.3.cloned.1.call-start = ((), (), s32[]{:S(2)}) async-start(), calls=%async_computation.6 | async-start | bytes 557056 | tf_op jit(solution)/shard_map/reduce_scatter | solution.py:107
  151.0 168.4 %reduce-scatter.5.cloned.1.call-start = ((), (), s32[]{:S(2)}) async-start(), calls=%async_computation.7 | async-start | bytes 557056 | tf_op jit(solution)/shard_map/reduce_scatter | solution.py:115
  154.3 80.2 %copy-start.8 = (bf16[512,256]{1,0:T(8,128)(2,1)S(1)}, bf16[512,256]{1,0:T(8,128)(2,1)}, u32[]{:S(2)}) copy-start(bf16[512,256]{1,0:T(8,128)(2,1)} %param.6) | copy-start | bytes 786436
  154.3 358.1 %all-reduce.5.cloned.1.call-start = ((), (), s32[]{:S(2)}) async-start(), calls=%async_computation.8 | async-start | bytes 3145728
  234.5 4.5 copy-start.5
Sparse Core Ops, SparseCore 0:
  151.1 81.9 reduce-scatter.2
  237.7 81.6 reduce-scatter.4
  322.4 189.9 all-reduce.4
